TPU v7x, 32 devices: a whole 2x2x4 slice. The times are simulated.
32 devices in a mesh: dp: 16 (over z, x, core), vocab: 2 (over y).
Axes of the slice: x: 2, y: 2, z: 4, core: 2. Of those that a mesh axis runs over, the one named last changes fastest.
Arguments:
- hidden: bfloat16 [2048, 8192], P('dp', 'vocab')
- rank_factor: bfloat16 [256, 8192], P(None, 'vocab'), may hold values from -0.0625 to 0.0625
- vocab_factor: bfloat16 [256, 77824], P('dp', 'vocab')
- lengths: int32 [2048], P('dp'), may hold values from 0 to 4096, as said below
- targets: int32 [2048], P('dp'), may hold values from 0 to 77823
- cotangent: bfloat16 [2048], P('dp'), may hold values from -96 to 96
- grammar: int32 [64, 22], P('dp', 'vocab'), may hold values from 0 to 1073741823, as said below
- assign: int32 [2048], P('dp'), may hold values from 0 to 127, as said below
Outputs:
- grad_hidden: bfloat16 [2048, 8192], P('dp', 'vocab')
- grad_factor: float32 [256, 8192], P('dp', 'vocab')
Inputs may be any that keep to these rules, and one draw needn't show every extreme that they name: `lengths`: in each aligned block of 128 rows the rows with a length above 0 come first; in every draw one such block has all 128 rows above 0 and a row of length 4096. `grammar`: only bits 0 to 29 of a word are used. `assign`: each aligned block of 128 entries is a permutation of 0 to 127.
All inputs are finite; a program needn't handle non-finite values.
Results may differ from a plain program's by a relative error of at most 0.0085.
Values may be sent and summed in bfloat16 or wider, within the bound.
No kernel may reach another device: no remote copies, remote signals or barrier semaphores. Data moves between devices by JAX's collectives and lax.ppermute only.
A program may use at most 128 MiB of HBM per device.

v0:
```python
import jax
import jax.numpy as jnp
from jax import lax
from jax.sharding import PartitionSpec as P

PREFIX_MAX = 4096
far_below = -1e30


def row_grads(hidden_rows, weight, target_rows, word_rows, live_count, rank_factor, factor, first):
    row_count = hidden_rows.shape[0]
    rank = rank_factor.shape[0]
    block_rows = min(128, row_count)
    width = factor.shape[1]
    tiles = width // 128
    partial_latent = lax.dot_general(
        hidden_rows, rank_factor, (((1,), (1,)), ((), ())), preferred_element_type=jnp.float32
    )
    latent = lax.psum(partial_latent, "vocab").astype(jnp.bfloat16)
    target_local = target_rows - first
    columns = jnp.arange(width, dtype=jnp.int32)
    shifts = jnp.arange(30, dtype=jnp.int32)
    blocks_live = (live_count + block_rows - 1) // block_rows

    def block_terms():
        logits = jnp.dot(latent, factor, preferred_element_type=jnp.float32)
        bits = jnp.right_shift(word_rows[:, :, None], shifts) & 1
        bits = bits.reshape(block_rows, -1)[:, :tiles]
        tile_on = jnp.broadcast_to((bits == 1)[:, :, None], (block_rows, tiles, 128)).reshape(
            block_rows, width
        )
        target_hit = columns[None, :] == target_local[:, None]
        allowed = tile_on | target_hit
        masked = jnp.where(allowed, logits, far_below)
        local_peak = jnp.max(masked, axis=1)
        peak = lax.pmax(local_peak, "vocab")
        powers = jnp.where(allowed, jnp.exp(masked - peak[:, None]), 0.0)
        total = lax.psum(jnp.sum(powers, axis=1), "vocab")
        row_probs = powers / total[:, None]
        score_grad = (weight[:, None] * (row_probs - target_hit.astype(jnp.float32))).astype(
            jnp.bfloat16
        )
        return lax.dot_general(
            score_grad, factor, (((1,), (1,)), ((), ())), preferred_element_type=jnp.float32
        )

    def step(index, carry):
        summed = lax.psum(block_terms(), "vocab").astype(jnp.bfloat16)
        return summed

    rank_grad = lax.fori_loop(0, blocks_live, step, jnp.zeros((row_count, rank), jnp.bfloat16))
    grad_rows = jnp.dot(rank_grad, rank_factor, preferred_element_type=jnp.float32).astype(
        jnp.bfloat16
    )
    return (rank_grad, grad_rows)


def body(hidden, rank_factor, vocab_factor, lengths, targets, cotangent, grammar, assign):
    row_count = hidden.shape[0]
    groups = lax.axis_size("dp")
    share = row_count // groups
    width = vocab_factor.shape[1]
    first = lax.axis_index("vocab") * width
    factor = lax.all_gather(vocab_factor, "dp", axis=0, tiled=True)
    row_words = jnp.repeat(grammar, row_count // grammar.shape[0], axis=0)
    weight = cotangent.astype(jnp.float32) * lengths.astype(jnp.float32) / PREFIX_MAX
    live_count = jnp.sum((lengths > 0).astype(jnp.int32))
    rank_used, grad_rows = row_grads(
        hidden, weight, targets, row_words, live_count, rank_factor, factor, first
    )
    picked = jnp.take(grad_rows, assign, axis=0).reshape(groups, share, -1)
    grad_hidden = lax.all_to_all(picked, "dp", split_axis=0, concat_axis=0, tiled=True).reshape(
        row_count, -1
    )
    grad_factor = lax.psum_scatter(
        lax.dot_general(
            rank_used, hidden, (((0,), (0,)), ((), ())), preferred_element_type=jnp.float32
        ),
        "dp",
        scatter_dimension=0,
        tiled=True,
    )
    return (grad_hidden, grad_factor)


def solution(mesh):
    return jax.shard_map(
        body,
        mesh=mesh,
        in_specs=(
            P("dp", "vocab"),
            P(None, "vocab"),
            P("dp", "vocab"),
            P("dp"),
            P("dp"),
            P("dp"),
            P("dp", "vocab"),
            P("dp"),
        ),
        out_specs=(P("dp", "vocab"), P("dp", "vocab")),
        check_vma=False,
    )
```

profile of v0, /device:TPU:0, one launch (start us, length us, event | category | flops | bytes accessed | tf_op | source)
XLA Modules:
  0.0 280.0 jit_solution(16738621352985855964)
XLA Ops:
  7.2 0.0 copy-start
  7.2 0.0 all-gather.2.cloned.1.call-start
  7.2 0.7 all-gather.2.cloned.1.call-update
  7.9 0.0 reduce-scatter.2.cloned.1.call-start
  8.0 1.3 fusion.6
  9.9 0.8 copy.10
  10.7 0.1 broadcast_in_dim.54
  10.8 0.1 shift_right_arithmetic.30
  10.9 0.1 shift_right_arithmetic.34
  11.0 0.1 fusion.3
  11.1 0.2 copy.11
  11.3 0.0 copy-done
  11.3 2.1 fusion.9
  13.4 11.4 %all-reduce.2 = bf16[128,256]{1,0:T(8,128)(2,1)S(1)} all-reduce(f32[128,256]{1,0:T(8,128)S(1)} %fusion.9), channel_id=1, replica_groups=mesh['dp'=16,'vocab'=2] {'vocab'}, use_global_device_ids=true, to_apply=%region_1.0 | all-reduce | flops 32768 | bytes 196608 | tf_op jit(solution)/shard_map/psum | solution.py:19
  24.8 0.7 broadcast_subtract_fusion
  25.5 0.7 multiply_multiply_fusion
  26.2 90.0 %all-gather.2.cloned.1.call-done = bf16[256,38912]{1,0:T(8,128)(2,1)} async-done(((bf16[16,38912]{1,0:T(8,128)(2,1)}), bf16[256,38912]{1,0:T(8,128)(2,1)}) %all-gather.2.cloned.1.call-update) | async-done | bytes 19922960 | tf_op jit(solution)/shard_map/all_gather | solution.py:64
  116.2 6.6 %broadcast_in_dim.55 = pred[128,304,128]{2,1,0:T(8,128)(4,1)S(1)} broadcast(pred[128,304]{1,0:T(8,128)(4,1)S(1)} %copy.11), dimensions={0,1} | broadcast | bytes 5019648 | tf_op jit(solution)/shard_map/while/body/broadcast_in_dim | solution.py:29
  122.9 0.0 copy-start.1
  122.9 17.7 %fusion = (f32[128]{0:T(128)S(1)}, f32[128,38912]{1,0:T(8,128)}) fusion(s32[128]{0:T(128)S(1)} %broadcast_subtract_fusion, s32[38912]{0:T(1024)S(1)} %add_bitcast_fusion, pred[16,8,304,128]{3,2,1,0:T(8,128)(4,1)S(1)} %bitcast.28, bf16[128,256]{1,0:T(8,128)(2,1)S(1)} %all-reduce.2, bf16[256,38912]{1,0:T(8,128)(2,1)} %all-gather.2.cloned.1.call-done), kind=kOutput, calls=%fused_computation.6 | convolution fusion | flops 2570059776 | bytes 45048832 | tf_op jit(solution)/shard_map/while/body/dot_general | solution.py:26
  140.6 0.0 copy-done.1
  140.6 4.9 %pmax.11 = f32[128]{0:T(128)S(1)} all-reduce(f32[128]{0:T(128)S(1)} %get-tuple-element.205), channel_id=1, replica_groups=mesh['dp'=16,'vocab'=2] {'vocab'}, use_global_device_ids=true, to_apply=%region_3.4 | all-reduce | flops 128 | bytes 1024 | tf_op jit(solution)/shard_map/while/body/pmax | solution.py:36
  145.5 15.0 %select_reduce_fusion = f32[128]{0:T(128)S(1)} fusion(f32[128]{0:T(128)S(1)} %pmax.11, f32[128,38912]{1,0:T(8,128)} %get-tuple-element.206, s32[128]{0:T(128)S(1)} %broadcast_subtract_fusion, s32[38912]{0:T(1024)S(1)} %add_bitcast_fusion, pred[16,8,304,128]{3,2,1,0:T(8,128)(4,1)} %bitcast.29), kind=kLoop, calls=%fused_computation.2 | loop fusion | flops 29884288 | bytes 25060864 | tf_op jit(solution)/shard_map/while/body/reduce_sum | solution.py:38
  160.5 5.1 %psum.32 = f32[128]{0:T(128)S(1)} all-reduce(f32[128]{0:T(128)S(1)} %select_reduce_fusion), channel_id=1, replica_groups=mesh['dp'=16,'vocab'=2] {'vocab'}, use_global_device_ids=true, to_apply=%region_5.6 | all-reduce | flops 128 | bytes 1024 | tf_op jit(solution)/shard_map/while/body/psum | solution.py:38
  165.6 0.0 copy-start.2
  165.6 0.0 copy-start.3
  165.7 18.5 %fusion.1 = f32[128,256]{1,0:T(8,128)S(1)} fusion(bf16[256,38912]{1,0:T(8,128)(2,1)} %all-gather.2.cloned.1.call-done, f32[128,38912]{1,0:T(8,128)} %get-tuple-element.206, pred[16,8,304,128]{3,2,1,0:T(8,128)(4,1)} %bitcast.30, f32[128]{0:T(128)S(1)} %psum.32, f32[128]{0:T(128)S(1)} %pmax.11, f32[128]{0:T(128)S(1)} %multiply_multiply_fusion, ...), kind=kOutput, calls=%fused_computation.7 | convolution fusion | flops 2599944192 | bytes 44959744 | tf_op jit(solution)/shard_map/while/body/dot_general | solution.py:43
  184.1 9.7 %all-reduce.3 = bf16[128,256]{1,0:T(8,128)(2,1)S(1)} all-reduce(f32[128,256]{1,0:T(8,128)S(1)} %fusion.1), channel_id=1, replica_groups=mesh['dp'=16,'vocab'=2] {'vocab'}, use_global_device_ids=true, to_apply=%region_6.7 | all-reduce | flops 32768 | bytes 196608 | tf_op jit(solution)/shard_map/while/body/psum | solution.py:48
  193.8 0.6 broadcast_in_dim.53
  194.5 0.6 while.16
  194.5 0.6 copy.27
  195.1 0.0 copy-done.2
  195.1 3.5 %fusion.10 = f32[256,4096]{1,0:T(8,128)} fusion(bf16[128,256]{1,0:T(8,128)(2,1)} %get-tuple-element.196, bf16[128,4096]{1,0:T(8,128)(2,1)S(1)} %copy-done.2), kind=kOutput, calls=%fused_computation.26 | convolution fusion | flops 268435456 | bytes 5308416 | tf_op jit(solution)/shard_map/dot_general | solution.py:76
  198.6 0.0 reduce-scatter.2.cloned.1.call-update
  198.6 0.0 copy-done.3
  198.7 0.1 broadcast_in_dim.51
  198.8 1.3 convolution_convert_fusion
  200.1 2.2 gather_fusion
  202.2 1.4 bitcast_select_fusion
  203.6 31.9 %all_to_all.5 = bf16[16,8,4096]{2,1,0:T(8,128)(2,1)S(1)} all-to-all(bf16[16,8,4096]{2,1,0:T(8,128)(2,1)S(1)} %bitcast_select_fusion), channel_id=1, replica_groups=mesh['dp'=16,'vocab'=2] {'dp'}, dimensions={0} | all-to-all | bytes 2097152 | tf_op jit(solution)/shard_map/all_to_all | solution.py:72
  235.5 36.7 %reduce-scatter.2.cloned.1.call-done = f32[16,4096]{1,0:T(8,128)} async-done(((f32[256,4096]{1,0:T(8,128)}), f32[16,4096]{1,0:T(8,128)}) %reduce-scatter.2.cloned.1.call-update) | async-done | bytes 262160 | tf_op jit(solution)/shard_map/reduce_scatter | solution.py:75
  272.2 1.0 copy.33
  (7 shorter events, 0.1 us)
Async XLA Ops:
  7.2 4.1 %copy-start = (bf16[256,4096]{1,0:T(8,128)(2,1)S(1)}, bf16[256,4096]{1,0:T(8,128)(2,1)}, u32[]{:S(2)}) copy-start(bf16[256,4096]{1,0:T(8,128)(2,1)} %param.11) | copy-start | bytes 6291460
  7.2 109.1 %all-gather.2.cloned.1.call-start = ((), (), s32[]{:S(2)}) async-start(), calls=%async_computation.2 | async-start | bytes 21168128 | tf_op jit(solution)/shard_map/all_gather | solution.py:64
  7.9 264.3 %reduce-scatter.2.cloned.1.call-start = ((), (), s32[]{:S(2)}) async-start(), calls=%async_computation.3 | async-start | bytes 4456448 | tf_op jit(solution)/shard_map/reduce_scatter | solution.py:75
  122.9 17.7 %copy-start.1 = (pred[128,304,128]{2,1,0:T(8,128)(4,1)}, pred[128,304,128]{2,1,0:T(8,128)(4,1)S(1)}, u32[]{:S(2)}) copy-start(pred[128,304,128]{2,1,0:T(8,128)(4,1)S(1)} %broadcast_in_dim.55) | copy-start | bytes 14942212
  165.6 29.5 %copy-start.2 = (bf16[128,4096]{1,0:T(8,128)(2,1)S(1)}, bf16[128,4096]{1,0:T(8,128)(2,1)}, u32[]{:S(2)}) copy-start(bf16[128,4096]{1,0:T(8,128)(2,1)} %param.10) | copy-start | bytes 3145732
  165.6 33.0 %copy-start.3 = (s32[128]{0:T(128)S(1)}, s32[128]{0:T(128)}, u32[]{:S(2)}) copy-start(s32[128]{0:T(128)} %param.17) | copy-start | bytes 1540
Sparse Core Ops, SparseCore 0:
  9.6 106.5 all-gather.1
  198.8 73.4 reduce-scatter.1
where the time goes:
time: 281 us; the launch traced here: 280 us
  waiting for transfers between devices  127 us (45%)
  blocking collectives  63.1 us (22%)
  matrix products  43 us (15%)
  other arithmetic  19.2 us (7%)
  between operations  14.9 us (5%)
  local copies, waits for them, and re-layouts  12.3 us (4%)
    all_gather x1, waiting for transfers between devices, body(): factor = lax.all_gather(vocab_factor, 'dp', axis=0, tiled=True)  90 us
    reduce_scatter x1, waiting for transfers between devices, body(): lax.psum_scatter(lax.dot_general(rank_used, hidden, (((0,), (0,)), ((), (...  36.7 us
    all_to_all x1, blocking collectives, body(): lax.all_to_all(picked, 'dp', split_axis=0, concat_axis=0, tiled=True)  31.9 us
    dot_general x1, matrix products, block_terms(): lax.dot_general(score_grad, factor, (((1,), (1,)), ((), ())), preferred_e...  18.5 us
    dot_general x1, matrix products, block_terms(): logits = jnp.dot(latent, factor, preferred_element_type=jnp.float32)  17.7 us
    reduce_sum x1, other arithmetic, block_terms(): total = lax.psum(jnp.sum(powers, axis=1), 'vocab')  15 us
    psum x1, blocking collectives, row_grads(): latent = lax.psum(partial_latent, 'vocab').astype(jnp.bfloat16)  11.4 us
    psum x1, blocking collectives, step(): summed = lax.psum(block_terms(), 'vocab').astype(jnp.bfloat16)  9.72 us
  transfers between devices with their start and end apart: 2, of which 2 were waited for; matrix products, arithmetic and copies ran while one was open for 4% of the time, Pallas kernels for 0%

commit v1 on v0

--- a/solution.py
+++ b/solution.py
@@ -5,6 +5,27 @@
 
 PREFIX_MAX = 4096
 far_below = -1e30
+
+
+def collect(array, axis, dim):
+    devices, mine, span = (lax.axis_size(axis), lax.axis_index(axis), array.shape[dim])
+    forward = [(i, (i + 1) % devices) for i in range(devices)]
+    left = [(i, (i - 1) % devices) for i in range(devices)]
+    whole = jnp.zeros((*array.shape[:dim], devices * span, *array.shape[dim + 1 :]), array.dtype)
+    whole = lax.dynamic_update_slice_in_dim(whole, array, mine * span, axis=dim)
+    from_left = from_right = array
+    half = devices // 2
+    for turn in range(1, half + 1):
+        from_left = lax.ppermute(from_left, axis, forward)
+        whole = lax.dynamic_update_slice_in_dim(
+            whole, from_left, (mine - turn) % devices * span, axis=dim
+        )
+        if turn < devices - half:
+            from_right = lax.ppermute(from_right, axis, left)
+            whole = lax.dynamic_update_slice_in_dim(
+                whole, from_right, (mine + turn) % devices * span, axis=dim
+            )
+    return whole
 
 
 def row_grads(hidden_rows, weight, target_rows, word_rows, live_count, rank_factor, factor, first):
@@ -61,7 +82,7 @@
     share = row_count // groups
     width = vocab_factor.shape[1]
     first = lax.axis_index("vocab") * width
-    factor = lax.all_gather(vocab_factor, "dp", axis=0, tiled=True)
+    factor = collect(vocab_factor, "dp", 0)
     row_words = jnp.repeat(grammar, row_count // grammar.shape[0], axis=0)
     weight = cotangent.astype(jnp.float32) * lengths.astype(jnp.float32) / PREFIX_MAX
     live_count = jnp.sum((lengths > 0).astype(jnp.int32))

time: 281 us -> 395 us (1.41)
  starting transfers between devices: 0.08 us -> 127 us
  waiting for transfers between devices: 127 us -> 82.3 us
  local copies, waits for them, and re-layouts: 12.3 us -> 40.5 us
  blocking collectives: 63.1 us -> 71.6 us
    ppermute x0 -> x15, starting transfers between devices: none -> 127 us  [the longest x8 119 us: collect(): from_left = lax.ppermute(from_left, axis, forward)]
    all_gather x1 -> x0, waiting for transfers between devices: 90 us -> none  [body(): factor = lax.all_gather(vocab_factor, 'dp', axis=0, tiled=True)]
    ppermute x0 -> x15, waiting for transfers between devices: none -> 45.1 us  [the longest x8 45.1 us: collect(): from_left = lax.ppermute(from_left, axis, forward)]
    dynamic_update_slice x0 -> x16, local copies, waits for them, and re-layouts: none -> 20.7 us  [the longest x8 10.2 us: collect(): lax.dynamic_update_slice_in_dim(whole, from_left, (mine - turn) % devices...]
    all_to_all x1, blocking collectives: 31.9 us -> 42 us  [body(): lax.all_to_all(picked, 'dp', split_axis=0, concat_axis=0, tiled=True)]
    broadcast_in_dim x0 -> x1, local copies, waits for them, and re-layouts: none -> 6.87 us  [collect(): jnp.zeros((*array.shape[:dim], devices * span, *array.shape[dim + 1:]), a...]
  transfers between devices with their start and end apart: 2 -> 16, of which waited for: 2 -> 8; matrix products, arithmetic and copies ran while one was open for 4% -> 9% of each run, Pallas kernels for 0% -> 0%
where the time goes in v1:
time: 395 us
  starting transfers between devices  127 us (32%)
  waiting for transfers between devices  82.3 us (21%)
  blocking collectives  71.6 us (18%)
  matrix products  41.8 us (11%)
  local copies, waits for them, and re-layouts  40.5 us (10%)
  other arithmetic  17.2 us (4%)
  between operations  14.9 us (4%)
    ppermute x8, starting transfers between devices, collect(): from_left = lax.ppermute(from_left, axis, forward)  119 us
    ppermute x8, waiting for transfers between devices, collect(): from_left = lax.ppermute(from_left, axis, forward)  45.1 us
    all_to_all x1, blocking collectives, body(): lax.all_to_all(picked, 'dp', split_axis=0, concat_axis=0, tiled=True)  42 us
    reduce_scatter x1, waiting for transfers between devices, body(): lax.psum_scatter(lax.dot_general(rank_used, hidden, (((0,), (0,)), ((), (...  37.2 us
    dot_general x1, matrix products, block_terms(): lax.dot_general(score_grad, factor, (((1,), (1,)), ((), ())), preferred_e...  18.4 us
    dot_general x1, matrix products, block_terms(): logits = jnp.dot(latent, factor, preferred_element_type=jnp.float32)  17.8 us
    reduce_sum x1, other arithmetic, block_terms(): total = lax.psum(jnp.sum(powers, axis=1), 'vocab')  15 us
    psum x1, blocking collectives, row_grads(): latent = lax.psum(partial_latent, 'vocab').astype(jnp.bfloat16)  10.6 us
  transfers between devices with their start and end apart: 16, of which 8 were waited for; matrix products, arithmetic and copies ran while one was open for 9% of the time, Pallas kernels for 0%

profile of v1, /device:TPU:0, one launch (start us, length us, event | category | flops | bytes accessed | tf_op | source)
XLA Modules:
  0.0 394.9 jit_solution(4924901909729411489)
XLA Ops:
  7.8 5.0 %collective-permute-start.1 = (bf16[16,38912]{1,0:T(8,128)(2,1)}, bf16[16,38912]{1,0:T(8,128)(2,1)}, u32[]{:S(2)}, u32[]{:S(2)}) collective-permute-start(bf16[16,38912]{1,0:T(8,128)(2,1)} %param.12), channel_id=1, source_target_pairs={{0,30},{2,0},{4,2},{6,4},{8,6},{10,8},{12,10},{14,12},{16,14},{18,... | collective-permute-start | bytes 3735560 | tf_op jit(solution)/shard_map/ppermute | solution.py:24
  13.9 6.9 %broadcast_in_dim.59 = bf16[256,38912]{1,0:T(8,128)(2,1)} broadcast(bf16[]{:T(256)} %constant.154.clone.1), dimensions={} | broadcast | bytes 19922946 | tf_op jit(solution)/shard_map/broadcast_in_dim | solution.py:14
  20.8 1.1 constant_dynamic-update-slice_fusion.15
  25.0 10.6 %all-reduce.2 = bf16[128,256]{1,0:T(8,128)(2,1)} all-reduce(f32[128,256]{1,0:T(8,128)S(1)} %fusion.9), channel_id=1, replica_groups=mesh['dp'=16,'vocab'=2] {'vocab'}, use_global_device_ids=true, to_apply=%region_1.2 | all-reduce | flops 32768 | bytes 196608 | tf_op jit(solution)/shard_map/psum | solution.py:40
  35.7 2.2 collective-permute-start.2
  37.9 2.3 collective-permute-start.3
  40.2 2.4 constant_dynamic-update-slice_fusion.14
  42.5 2.4 constant_dynamic-update-slice_fusion.13
  45.0 10.1 %collective-permute-done.2 = bf16[16,38912]{1,0:T(8,128)(2,1)S(1)} collective-permute-done((bf16[16,38912]{1,0:T(8,128)(2,1)}, bf16[16,38912]{1,0:T(8,128)(2,1)S(1)}, u32[]{:S(2)}, u32[]{:S(2)}) %collective-permute-start.2) | collective-permute-done | bytes 1245216 | tf_op jit(solution)/shard_map/ppermute | solution.py:19
  55.1 12.0 %collective-permute-start.4 = (bf16[16,38912]{1,0:T(8,128)(2,1)S(1)}, bf16[16,38912]{1,0:T(8,128)(2,1)S(1)}, u32[]{:S(2)}, u32[]{:S(2)}) collective-permute-start(bf16[16,38912]{1,0:T(8,128)(2,1)S(1)} %collective-permute-done.2), channel_id=1, source_target_pairs={{0,2},{2,4},{4,6},{6,8},{8,10},{10,12},{12,14},{14,16},{16,18},{18... | collective-permute-start | bytes 3735560 | tf_op jit(solution)/shard_map/ppermute | solution.py:19
  67.1 1.1 constant_dynamic-update-slice_fusion.12
  68.2 1.1 constant_dynamic-update-slice_fusion.11
  69.4 5.9 %collective-permute-done.4 = bf16[16,38912]{1,0:T(8,128)(2,1)S(1)} collective-permute-done((bf16[16,38912]{1,0:T(8,128)(2,1)S(1)}, bf16[16,38912]{1,0:T(8,128)(2,1)S(1)}, u32[]{:S(2)}, u32[]{:S(2)}) %collective-permute-start.4) | collective-permute-done | bytes 1245216 | tf_op jit(solution)/shard_map/ppermute | solution.py:19
  75.2 20.8 %collective-permute-start.6 = (bf16[16,38912]{1,0:T(8,128)(2,1)S(1)}, bf16[16,38912]{1,0:T(8,128)(2,1)S(1)}, u32[]{:S(2)}, u32[]{:S(2)}) collective-permute-start(bf16[16,38912]{1,0:T(8,128)(2,1)S(1)} %collective-permute-done.4), channel_id=1, source_target_pairs={{0,2},{2,4},{4,6},{6,8},{8,10},{10,12},{12,14},{14,16},{16,18},{18... | collective-permute-start | bytes 3735560 | tf_op jit(solution)/shard_map/ppermute | solution.py:19
  96.0 1.1 constant_dynamic-update-slice_fusion.10
  97.1 1.1 constant_dynamic-update-slice_fusion.9
  98.3 4.4 %collective-permute-done.6 = bf16[16,38912]{1,0:T(8,128)(2,1)S(1)} collective-permute-done((bf16[16,38912]{1,0:T(8,128)(2,1)S(1)}, bf16[16,38912]{1,0:T(8,128)(2,1)S(1)}, u32[]{:S(2)}, u32[]{:S(2)}) %collective-permute-start.6) | collective-permute-done | bytes 1245216 | tf_op jit(solution)/shard_map/ppermute | solution.py:19
  102.7 22.2 %collective-permute-start.8 = (bf16[16,38912]{1,0:T(8,128)(2,1)S(1)}, bf16[16,38912]{1,0:T(8,128)(2,1)S(1)}, u32[]{:S(2)}, u32[]{:S(2)}) collective-permute-start(bf16[16,38912]{1,0:T(8,128)(2,1)S(1)} %collective-permute-done.6), channel_id=1, source_target_pairs={{0,2},{2,4},{4,6},{6,8},{8,10},{10,12},{12,14},{14,16},{16,18},{18... | collective-permute-start | bytes 3735560 | tf_op jit(solution)/shard_map/ppermute | solution.py:19
  124.9 1.1 constant_dynamic-update-slice_fusion.8
  126.0 1.2 constant_dynamic-update-slice_fusion.7
  127.2 5.0 %collective-permute-done.8 = bf16[16,38912]{1,0:T(8,128)(2,1)S(1)} collective-permute-done((bf16[16,38912]{1,0:T(8,128)(2,1)S(1)}, bf16[16,38912]{1,0:T(8,128)(2,1)S(1)}, u32[]{:S(2)}, u32[]{:S(2)}) %collective-permute-start.8) | collective-permute-done | bytes 1245216 | tf_op jit(solution)/shard_map/ppermute | solution.py:19
  132.2 22.3 %collective-permute-start.10 = (bf16[16,38912]{1,0:T(8,128)(2,1)S(1)}, bf16[16,38912]{1,0:T(8,128)(2,1)S(1)}, u32[]{:S(2)}, u32[]{:S(2)}) collective-permute-start(bf16[16,38912]{1,0:T(8,128)(2,1)S(1)} %collective-permute-done.8), channel_id=1, source_target_pairs={{0,2},{2,4},{4,6},{6,8},{8,10},{10,12},{12,14},{14,16},{16,18},{18... | collective-permute-start | bytes 3735560 | tf_op jit(solution)/shard_map/ppermute | solution.py:19
  154.5 1.1 constant_dynamic-update-slice_fusion.6
  155.6 1.1 constant_dynamic-update-slice_fusion.5
  156.7 5.0 %collective-permute-done.10 = bf16[16,38912]{1,0:T(8,128)(2,1)S(1)} collective-permute-done((bf16[16,38912]{1,0:T(8,128)(2,1)S(1)}, bf16[16,38912]{1,0:T(8,128)(2,1)S(1)}, u32[]{:S(2)}, u32[]{:S(2)}) %collective-permute-start.10) | collective-permute-done | bytes 1245216 | tf_op jit(solution)/shard_map/ppermute | solution.py:19
  161.7 19.6 %collective-permute-start.12 = (bf16[16,38912]{1,0:T(8,128)(2,1)S(1)}, bf16[16,38912]{1,0:T(8,128)(2,1)S(1)}, u32[]{:S(2)}, u32[]{:S(2)}) collective-permute-start(bf16[16,38912]{1,0:T(8,128)(2,1)S(1)} %collective-permute-done.10), channel_id=1, source_target_pairs={{0,2},{2,4},{4,6},{6,8},{8,10},{10,12},{12,14},{14,16},{16,18},{18... | collective-permute-start | bytes 3735560 | tf_op jit(solution)/shard_map/ppermute | solution.py:19
  181.4 1.1 constant_dynamic-update-slice_fusion.4
  182.5 1.1 constant_dynamic-update-slice_fusion.3
  183.6 7.1 %collective-permute-done.12 = bf16[16,38912]{1,0:T(8,128)(2,1)S(1)} collective-permute-done((bf16[16,38912]{1,0:T(8,128)(2,1)S(1)}, bf16[16,38912]{1,0:T(8,128)(2,1)S(1)}, u32[]{:S(2)}, u32[]{:S(2)}) %collective-permute-start.12) | collective-permute-done | bytes 1245216 | tf_op jit(solution)/shard_map/ppermute | solution.py:19
  190.7 19.5 %collective-permute-start.14 = (bf16[16,38912]{1,0:T(8,128)(2,1)S(1)}, bf16[16,38912]{1,0:T(8,128)(2,1)S(1)}, u32[]{:S(2)}, u32[]{:S(2)}) collective-permute-start(bf16[16,38912]{1,0:T(8,128)(2,1)S(1)} %collective-permute-done.12), channel_id=1, source_target_pairs={{0,2},{2,4},{4,6},{6,8},{8,10},{10,12},{12,14},{14,16},{16,18},{18... | collective-permute-start | bytes 3735560 | tf_op jit(solution)/shard_map/ppermute | solution.py:19
  210.3 1.1 constant_dynamic-update-slice_fusion.2
  211.4 1.2 constant_dynamic-update-slice_fusion.1
  212.5 7.7 %collective-permute-done.14 = bf16[16,38912]{1,0:T(8,128)(2,1)S(1)} collective-permute-done((bf16[16,38912]{1,0:T(8,128)(2,1)S(1)}, bf16[16,38912]{1,0:T(8,128)(2,1)S(1)}, u32[]{:S(2)}, u32[]{:S(2)}) %collective-permute-start.14) | collective-permute-done | bytes 1245216 | tf_op jit(solution)/shard_map/ppermute | solution.py:19
  220.2 1.1 constant_dynamic-update-slice_fusion
  221.3 6.6 %broadcast_in_dim.58 = pred[128,304,128]{2,1,0:T(8,128)(4,1)S(1)} broadcast(pred[128,304]{1,0:T(8,128)(4,1)S(1)} %copy-done.4), dimensions={0,1} | broadcast | bytes 5019648 | tf_op jit(solution)/shard_map/while/body/broadcast_in_dim | solution.py:50
  228.0 17.8 %fusion = (f32[128]{0:T(128)S(1)}, f32[128,38912]{1,0:T(8,128)}) fusion(s32[128]{0:T(128)S(1)} %broadcast_subtract_fusion, s32[38912]{0:T(1024)S(1)} %add_bitcast_fusion, pred[16,8,304,128]{3,2,1,0:T(8,128)(4,1)S(1)} %bitcast.28, bf16[128,256]{1,0:T(8,128)(2,1)} %all-reduce.2, bf16[256,38912]{1,0:T(8,128)(2,1)} %constant_dynamic-update-slice_fusion), kind=kOutput, calls=%fused_computation.6 | convolution fusion | flops 2570059776 | bytes 45048832 | tf_op jit(solution)/shard_map/while/body/dot_general | solution.py:47
  245.7 4.9 %pmax.11 = f32[128]{0:T(128)S(1)} all-reduce(f32[128]{0:T(128)S(1)} %get-tuple-element.205), channel_id=1, replica_groups=mesh['dp'=16,'vocab'=2] {'vocab'}, use_global_device_ids=true, to_apply=%region_3.4 | all-reduce | flops 128 | bytes 1024 | tf_op jit(solution)/shard_map/while/body/pmax | solution.py:57
  250.6 15.0 %select_reduce_fusion = f32[128]{0:T(128)S(1)} fusion(f32[128]{0:T(128)S(1)} %pmax.11, f32[128,38912]{1,0:T(8,128)} %get-tuple-element.206, s32[128]{0:T(128)S(1)} %broadcast_subtract_fusion, s32[38912]{0:T(1024)S(1)} %add_bitcast_fusion, pred[16,8,304,128]{3,2,1,0:T(8,128)(4,1)} %bitcast.29), kind=kLoop, calls=%fused_computation.2 | loop fusion | flops 29884288 | bytes 25060864 | tf_op jit(solution)/shard_map/while/body/reduce_sum | solution.py:59
  265.6 5.1 %psum.32 = f32[128]{0:T(128)S(1)} all-reduce(f32[128]{0:T(128)S(1)} %select_reduce_fusion), channel_id=1, replica_groups=mesh['dp'=16,'vocab'=2] {'vocab'}, use_global_device_ids=true, to_apply=%region_5.6 | all-reduce | flops 128 | bytes 1024 | tf_op jit(solution)/shard_map/while/body/psum | solution.py:59
  270.8 18.4 %fusion.1 = f32[128,256]{1,0:T(8,128)S(1)} fusion(bf16[256,38912]{1,0:T(8,128)(2,1)} %constant_dynamic-update-slice_fusion, f32[128,38912]{1,0:T(8,128)} %get-tuple-element.206, pred[16,8,304,128]{3,2,1,0:T(8,128)(4,1)} %bitcast.30, f32[128]{0:T(128)S(1)} %psum.32, f32[128]{0:T(128)S(1)} %pmax.11, f32[128]{0:T(128)S(1)} %multiply_multiply_fusion, ...), kind=kOutput, calls=%fused_computation.7 | convolution fusion | flops 2599944192 | bytes 44959744 | tf_op jit(solution)/shard_map/while/body/dot_general | solution.py:64
  289.2 8.9 %all-reduce.3 = bf16[128,256]{1,0:T(8,128)(2,1)S(1)} all-reduce(f32[128,256]{1,0:T(8,128)S(1)} %fusion.1), channel_id=1, replica_groups=mesh['dp'=16,'vocab'=2] {'vocab'}, use_global_device_ids=true, to_apply=%region_6.7 | all-reduce | flops 32768 | bytes 196608 | tf_op jit(solution)/shard_map/while/body/psum | solution.py:69
  299.4 3.5 fusion.10
  303.1 1.3 convolution_convert_fusion
  304.3 2.2 gather_fusion
  306.5 1.4 bitcast_select_fusion
  307.9 42.0 %all_to_all.5 = bf16[16,8,4096]{2,1,0:T(8,128)(2,1)S(1)} all-to-all(bf16[16,8,4096]{2,1,0:T(8,128)(2,1)S(1)} %bitcast_select_fusion), channel_id=1, replica_groups=mesh['dp'=16,'vocab'=2] {'dp'}, dimensions={0} | all-to-all | bytes 2097152 | tf_op jit(solution)/shard_map/all_to_all | solution.py:93
  349.9 37.2 %reduce-scatter.2.cloned.1.call-done = f32[16,4096]{1,0:T(8,128)} async-done(((f32[256,4096]{1,0:T(8,128)}), f32[16,4096]{1,0:T(8,128)}) %reduce-scatter.2.cloned.1.call-update) | async-done | bytes 262160 | tf_op jit(solution)/shard_map/reduce_scatter | solution.py:96
  387.1 1.0 copy.49
  (55 shorter events, 6.1 us)
Async XLA Ops:
  7.2 14.9 %copy-start = (bf16[256,4096]{1,0:T(8,128)(2,1)S(1)}, bf16[256,4096]{1,0:T(8,128)(2,1)}, u32[]{:S(2)}) copy-start(bf16[256,4096]{1,0:T(8,128)(2,1)} %param.11) | copy-start | bytes 6291460
  7.2 14.9 %copy-start.2 = (bf16[128,4096]{1,0:T(8,128)(2,1)S(1)}, bf16[128,4096]{1,0:T(8,128)(2,1)}, u32[]{:S(2)}) copy-start(bf16[128,4096]{1,0:T(8,128)(2,1)} %param.10) | copy-start | bytes 3145732
  7.2 15.7 %copy-start.6 = (s32[128]{0:T(128)S(1)}, s32[128]{0:T(128)}, u32[]{:S(2)}) copy-start(s32[128]{0:T(128)} %param.13) | copy-start | bytes 1540
  7.2 28.4 %copy-start.5 = (s32[128]{0:T(128)S(1)}, s32[128]{0:T(128)}, u32[]{:S(2)}) copy-start(s32[128]{0:T(128)} %param.14) | copy-start | bytes 1540
  7.2 28.4 %copy-start.7 = (bf16[128]{0:T(256)(128)(2,1)S(1)}, bf16[128]{0:T(256)(128)(2,1)}, u32[]{:S(2)}) copy-start(bf16[128]{0:T(256)(128)(2,1)} %param.15) | copy-start | bytes 772
  7.2 379.9 %reduce-scatter.2.cloned.1.call-start = ((), (), s32[]{:S(2)}) async-start(), calls=%async_computation.2 | async-start | bytes 4456448 | tf_op jit(solution)/shard_map/reduce_scatter | solution.py:96
  7.3 28.4 %collective-permute-start = (bf16[16,38912]{1,0:T(8,128)(2,1)}, bf16[16,38912]{1,0:T(8,128)(2,1)}, u32[]{:S(2)}, u32[]{:S(2)}) collective-permute-start(bf16[16,38912]{1,0:T(8,128)(2,1)} %param.12), channel_id=1, source_target_pairs={{0,2},{2,4},{4,6},{6,8},{8,10},{10,12},{12,14},{14,16},{16,18},{18... | collective-permute-start | bytes 3735560 | tf_op jit(solution)/shard_map/ppermute | solution.py:19
  7.8 30.1 %collective-permute-start.1 = (bf16[16,38912]{1,0:T(8,128)(2,1)}, bf16[16,38912]{1,0:T(8,128)(2,1)}, u32[]{:S(2)}, u32[]{:S(2)}) collective-permute-start(bf16[16,38912]{1,0:T(8,128)(2,1)} %param.12), channel_id=1, source_target_pairs={{0,30},{2,0},{4,2},{6,4},{8,6},{10,8},{12,10},{14,12},{16,14},{18,... | collective-permute-start | bytes 3735560 | tf_op jit(solution)/shard_map/ppermute | solution.py:24
  13.9 6.9 %copy-start.3 = (bf16[16,38912]{1,0:T(8,128)(2,1)S(1)}, bf16[16,38912]{1,0:T(8,128)(2,1)}, u32[]{:S(2)}) copy-start(bf16[16,38912]{1,0:T(8,128)(2,1)} %param.12) | copy-start | bytes 3735556
  35.6 185.7 %copy-start.4 = (pred[128,304]{1,0:T(8,128)(4,1)S(1)}, pred[128,304]{1,0:T(8,128)(4,1)}, u32[]{:S(2)}) copy-start(pred[128,304]{1,0:T(8,128)(4,1)} %copy.11) | copy-start | bytes 116740
  35.7 19.4 %collective-permute-start.2 = (bf16[16,38912]{1,0:T(8,128)(2,1)}, bf16[16,38912]{1,0:T(8,128)(2,1)S(1)}, u32[]{:S(2)}, u32[]{:S(2)}) collective-permute-start(bf16[16,38912]{1,0:T(8,128)(2,1)} %collective-permute-done), channel_id=1, source_target_pairs={{0,2},{2,4},{4,6},{6,8},{8,10},{10,12},{12,14},{14,16},{16,18},{18... | collective-permute-start | bytes 3735560 | tf_op jit(solution)/shard_map/ppermute | solution.py:19
  37.9 29.2 %collective-permute-start.3 = (bf16[16,38912]{1,0:T(8,128)(2,1)}, bf16[16,38912]{1,0:T(8,128)(2,1)S(1)}, u32[]{:S(2)}, u32[]{:S(2)}) collective-permute-start(bf16[16,38912]{1,0:T(8,128)(2,1)} %collective-permute-done.1), channel_id=1, source_target_pairs={{0,30},{2,0},{4,2},{6,4},{8,6},{10,8},{12,10},{14,12},{16,14},{18,... | collective-permute-start | bytes 3735560 | tf_op jit(solution)/shard_map/ppermute | solution.py:24
  55.1 20.2 %collective-permute-start.4 = (bf16[16,38912]{1,0:T(8,128)(2,1)S(1)}, bf16[16,38912]{1,0:T(8,128)(2,1)S(1)}, u32[]{:S(2)}, u32[]{:S(2)}) collective-permute-start(bf16[16,38912]{1,0:T(8,128)(2,1)S(1)} %collective-permute-done.2), channel_id=1, source_target_pairs={{0,2},{2,4},{4,6},{6,8},{8,10},{10,12},{12,14},{14,16},{16,18},{18... | collective-permute-start | bytes 3735560 | tf_op jit(solution)/shard_map/ppermute | solution.py:19
  67.1 28.9 %collective-permute-start.5 = (bf16[16,38912]{1,0:T(8,128)(2,1)S(1)}, bf16[16,38912]{1,0:T(8,128)(2,1)S(1)}, u32[]{:S(2)}, u32[]{:S(2)}) collective-permute-start(bf16[16,38912]{1,0:T(8,128)(2,1)S(1)} %collective-permute-done.3), channel_id=1, source_target_pairs={{0,30},{2,0},{4,2},{6,4},{8,6},{10,8},{12,10},{14,12},{16,14},{18,... | collective-permute-start | bytes 3735560 | tf_op jit(solution)/shard_map/ppermute | solution.py:24
  75.2 27.4 %collective-permute-start.6 = (bf16[16,38912]{1,0:T(8,128)(2,1)S(1)}, bf16[16,38912]{1,0:T(8,128)(2,1)S(1)}, u32[]{:S(2)}, u32[]{:S(2)}) collective-permute-start(bf16[16,38912]{1,0:T(8,128)(2,1)S(1)} %collective-permute-done.4), channel_id=1, source_target_pairs={{0,2},{2,4},{4,6},{6,8},{8,10},{10,12},{12,14},{14,16},{16,18},{18... | collective-permute-start | bytes 3735560 | tf_op jit(solution)/shard_map/ppermute | solution.py:19
  96.0 28.9 %collective-permute-start.7 = (bf16[16,38912]{1,0:T(8,128)(2,1)S(1)}, bf16[16,38912]{1,0:T(8,128)(2,1)S(1)}, u32[]{:S(2)}, u32[]{:S(2)}) collective-permute-start(bf16[16,38912]{1,0:T(8,128)(2,1)S(1)} %collective-permute-done.5), channel_id=1, source_target_pairs={{0,30},{2,0},{4,2},{6,4},{8,6},{10,8},{12,10},{14,12},{16,14},{18,... | collective-permute-start | bytes 3735560 | tf_op jit(solution)/shard_map/ppermute | solution.py:24
  102.7 29.5 %collective-permute-start.8 = (bf16[16,38912]{1,0:T(8,128)(2,1)S(1)}, bf16[16,38912]{1,0:T(8,128)(2,1)S(1)}, u32[]{:S(2)}, u32[]{:S(2)}) collective-permute-start(bf16[16,38912]{1,0:T(8,128)(2,1)S(1)} %collective-permute-done.6), channel_id=1, source_target_pairs={{0,2},{2,4},{4,6},{6,8},{8,10},{10,12},{12,14},{14,16},{16,18},{18... | collective-permute-start | bytes 3735560 | tf_op jit(solution)/shard_map/ppermute | solution.py:19
  124.9 29.6 %collective-permute-start.9 = (bf16[16,38912]{1,0:T(8,128)(2,1)S(1)}, bf16[16,38912]{1,0:T(8,128)(2,1)S(1)}, u32[]{:S(2)}, u32[]{:S(2)}) collective-permute-start(bf16[16,38912]{1,0:T(8,128)(2,1)S(1)} %collective-permute-done.7), channel_id=1, source_target_pairs={{0,30},{2,0},{4,2},{6,4},{8,6},{10,8},{12,10},{14,12},{16,14},{18,... | collective-permute-start | bytes 3735560 | tf_op jit(solution)/shard_map/ppermute | solution.py:24
  132.2 29.5 %collective-permute-start.10 = (bf16[16,38912]{1,0:T(8,128)(2,1)S(1)}, bf16[16,38912]{1,0:T(8,128)(2,1)S(1)}, u32[]{:S(2)}, u32[]{:S(2)}) collective-permute-start(bf16[16,38912]{1,0:T(8,128)(2,1)S(1)} %collective-permute-done.8), channel_id=1, source_target_pairs={{0,2},{2,4},{4,6},{6,8},{8,10},{10,12},{12,14},{14,16},{16,18},{18... | collective-permute-start | bytes 3735560 | tf_op jit(solution)/shard_map/ppermute | solution.py:19
  154.5 26.9 %collective-permute-start.11 = (bf16[16,38912]{1,0:T(8,128)(2,1)S(1)}, bf16[16,38912]{1,0:T(8,128)(2,1)S(1)}, u32[]{:S(2)}, u32[]{:S(2)}) collective-permute-start(bf16[16,38912]{1,0:T(8,128)(2,1)S(1)} %collective-permute-done.9), channel_id=1, source_target_pairs={{0,30},{2,0},{4,2},{6,4},{8,6},{10,8},{12,10},{14,12},{16,14},{18,... | collective-permute-start | bytes 3735560 | tf_op jit(solution)/shard_map/ppermute | solution.py:24
  161.7 29.0 %collective-permute-start.12 = (bf16[16,38912]{1,0:T(8,128)(2,1)S(1)}, bf16[16,38912]{1,0:T(8,128)(2,1)S(1)}, u32[]{:S(2)}, u32[]{:S(2)}) collective-permute-start(bf16[16,38912]{1,0:T(8,128)(2,1)S(1)} %collective-permute-done.10), channel_id=1, source_target_pairs={{0,2},{2,4},{4,6},{6,8},{8,10},{10,12},{12,14},{14,16},{16,18},{18... | collective-permute-start | bytes 3735560 | tf_op jit(solution)/shard_map/ppermute | solution.py:19
  181.4 30.0 %collective-permute-start.13 = (bf16[16,38912]{1,0:T(8,128)(2,1)S(1)}, bf16[16,38912]{1,0:T(8,128)(2,1)S(1)}, u32[]{:S(2)}, u32[]{:S(2)}) collective-permute-start(bf16[16,38912]{1,0:T(8,128)(2,1)S(1)} %collective-permute-done.11), channel_id=1, source_target_pairs={{0,30},{2,0},{4,2},{6,4},{8,6},{10,8},{12,10},{14,12},{16,14},{18,... | collective-permute-start | bytes 3735560 | tf_op jit(solution)/shard_map/ppermute | solution.py:24
  190.7 29.5 %collective-permute-start.14 = (bf16[16,38912]{1,0:T(8,128)(2,1)S(1)}, bf16[16,38912]{1,0:T(8,128)(2,1)S(1)}, u32[]{:S(2)}, u32[]{:S(2)}) collective-permute-start(bf16[16,38912]{1,0:T(8,128)(2,1)S(1)} %collective-permute-done.12), channel_id=1, source_target_pairs={{0,2},{2,4},{4,6},{6,8},{8,10},{10,12},{12,14},{14,16},{16,18},{18... | collective-permute-start | bytes 3735560 | tf_op jit(solution)/shard_map/ppermute | solution.py:19
  227.9 17.8 %copy-start.1 = (pred[128,304,128]{2,1,0:T(8,128)(4,1)}, pred[128,304,128]{2,1,0:T(8,128)(4,1)S(1)}, u32[]{:S(2)}) copy-start(pred[128,304,128]{2,1,0:T(8,128)(4,1)S(1)} %broadcast_in_dim.58) | copy-start | bytes 14942212
  270.8 32.1 %copy-start.8 = (s32[128]{0:T(128)S(1)}, s32[128]{0:T(128)}, u32[]{:S(2)}) copy-start(s32[128]{0:T(128)} %param.17) | copy-start | bytes 1540
Sparse Core Ops, SparseCore 0:
  303.0 84.0 reduce-scatter.1
